TPU v7x, 256 devices: a whole 4x4x8 slice. The times are simulated.
256 devices in a mesh: tok: 32 (over x, z), head: 8 (over y, core).
Axes of the slice: x: 4, y: 4, z: 8, core: 2. Of those that a mesh axis runs over, the one named last changes fastest.
Arguments:
- tokens: bfloat16 [32768, 1664], P(('tok', 'head')), may hold values from -75 to 75
- attn_gain: float32 [1664], replicated, may hold values from 0.1 to 1.9
- qkv_weight: bfloat16 [3, 1664, 1664], P(None, 'head'), may hold values from -5 to 5
- out_weight: bfloat16 [1664, 1664], P('head'), may hold values from -0.4375 to 0.4375
- merge_gain: float32 [1664], replicated, may hold values from 0.1 to 1.9
- merge_weight: bfloat16 [6656, 4096], P('head', 'tok'), may hold values from -0.078125 to 0.078125
- grid_sizes: int32 [2, 128], P(None, 'tok'), may hold values from 2 to 16, as said below
- segment_ids: int32 [32768], P('tok'), may hold values from 0 to 127, as said below
- patch_pos: int32 [2, 32768], P(None, 'tok'), may hold values from 0 to 15, as said below
- live_mask: int32 [32768], P('tok'), may hold values from 0 to 1, as said below
- owners: int32 [8192, 1], P(('tok', 'head')), may hold values from 0 to 31; in each aligned block of 32 rows (0 to 31, 32 to 63, ...) at most 2 rows name the same one
Outputs:
- delivered: bfloat16 [16384, 4096], P(('tok', 'head'))
Inputs may be any that keep to these rules, and one draw needn't show every extreme that they name: `grid_sizes`: both sides of every image are even, and some image is 16 by 16. `segment_ids`: never fall along the tokens. The aligned block b of 1024 tokens holds images b * 4 to (b + 1) * 4 - 1 packed in order from the block's start, image s taking grid_sizes[0, s] * grid_sizes[1, s] tokens; the block's remaining tokens carry the number of its last image. `patch_pos`: an image's tokens come in 2x2 windows, windows in row-major order, each window as (2 * r, 2 * c), (2 * r, 2 * c + 1), (2 * r + 1, 2 * c), (2 * r + 1, 2 * c + 1); padding tokens sit at (0, 0). `live_mask`: 1 exactly on the tokens that belong to an image. `owners`: in each aligned block of 32 rows (the merged rows of one device) no owner is named more than 2 times.
All inputs are finite; a program needn't handle non-finite values.
Results may differ from a plain program's by a relative error of at most 0.024.
Values may be sent and summed in bfloat16 or wider, within the bound.
No kernel may reach another device: no remote copies, remote signals or barrier semaphores. Data moves between devices by JAX's collectives and lax.ppermute only.
A program may use at most 64 MiB of HBM per device.

v0:
```python
import jax
import jax.numpy as jnp
from jax import lax
from jax.sharding import PartitionSpec as P

D = 1664
HD = 104
SIDE = 16
TOK = ("tx", "tz")
HEAD = ("hy", "hc")
Z_SIZE = 8
EPSILON = 1e-06
NEGATIVE = -1e30


def layer_norm(values, gain_vec):
    average = jnp.mean(values, axis=-1, keepdims=True)
    centred = values - average
    variance = jnp.mean(centred * centred, axis=-1, keepdims=True)
    return centred * lax.rsqrt(variance + EPSILON) * gain_vec


def rotate(vectors, row_coord, col_coord):
    quarter = vectors.shape[-1] // 4
    frequency = 10000.0 ** (-jnp.arange(quarter, dtype=jnp.float32) / quarter)
    pieces = []
    for which_axis, coordinate in ((0, row_coord), (1, col_coord)):
        leading = vectors[..., 2 * which_axis * quarter : (2 * which_axis + 1) * quarter]
        trailing = vectors[..., (2 * which_axis + 1) * quarter : (2 * which_axis + 2) * quarter]
        angles = coordinate[:, None, None] * frequency
        cosine = jnp.cos(angles)
        sine_val = jnp.sin(angles)
        pieces.append(leading * cosine - trailing * sine_val)
        pieces.append(leading * sine_val + trailing * cosine)
    return jnp.concatenate(pieces, axis=-1)


def body(
    tokens,
    attn_gain,
    qkv_weight,
    out_weight,
    merge_gain,
    merge_weight,
    grid_sizes,
    segment_ids,
    patch_pos,
    live_mask,
    owners,
):
    group_len = segment_ids.shape[0]
    local_rows = tokens.shape[0]
    head_width = qkv_weight.shape[1]
    heads_here = head_width // HD
    tok_count = lax.axis_size("tx") * lax.axis_size("tz")
    image_count = grid_sizes.shape[1]
    local_image = (
        segment_ids
        - (lax.axis_index("tx") * lax.axis_size("tz") + lax.axis_index("tz")) * image_count
    )
    image_match = local_image[:, None] == jnp.arange(image_count, dtype=jnp.int32)[None, :]
    grid_float = grid_sizes.astype(jnp.float32)
    row_size = jnp.sum(jnp.where(image_match, grid_float[0][None, :], 0.0), axis=1)
    col_size = jnp.sum(jnp.where(image_match, grid_float[1][None, :], 0.0), axis=1)
    row_coord = patch_pos[0].astype(jnp.float32) * SIDE / row_size
    col_coord = patch_pos[1].astype(jnp.float32) * SIDE / col_size
    stacked_weight = qkv_weight.reshape(3 * head_width, D)
    normed = layer_norm(tokens.astype(jnp.float32), attn_gain).astype(jnp.bfloat16)
    projected_rows = lax.dot_general(
        lax.all_gather(normed, HEAD, axis=0, tiled=True),
        stacked_weight,
        (((1,), (1,)), ((), ())),
        preferred_element_type=jnp.float32,
    )
    projected_rows = projected_rows.reshape(group_len, 3, heads_here, HD)
    query_all = (rotate(projected_rows[:, 0], row_coord, col_coord) * HD ** (-0.5)).astype(
        jnp.bfloat16
    )
    key_all = rotate(projected_rows[:, 1], row_coord, col_coord).astype(jnp.bfloat16)
    value_all = projected_rows[:, 2].astype(jnp.bfloat16)
    block_len = min(512, group_len)
    block_count = group_len // block_len
    key_live = live_mask == 1

    def allowed_pairs(query_start, span):
        query_seg = lax.dynamic_slice_in_dim(segment_ids, query_start, block_len)
        query_place = query_start + jnp.arange(block_len, dtype=jnp.int32)
        key_place = jnp.arange(span, dtype=jnp.int32)
        same_image = query_seg[:, None] == segment_ids[None, :]
        return same_image & (key_live[None, :] | (query_place[:, None] == key_place[None, :]))

    def query_block(query_start):
        queries = lax.dynamic_slice_in_dim(query_all, query_start, block_len, 0)
        allowed = allowed_pairs(query_start, group_len)
        scores = jnp.einsum("qhd,khd->hqk", queries, key_all, preferred_element_type=jnp.float32)
        masked = jnp.where(allowed[None], scores, NEGATIVE)
        row_top = jnp.max(masked, axis=2, keepdims=True)
        exponent = jnp.where(allowed[None], jnp.exp(masked - row_top), 0.0)
        denominator = jnp.sum(exponent, axis=2)
        numerator = jnp.einsum(
            "hqk,khd->qhd",
            exponent.astype(jnp.bfloat16),
            value_all,
            preferred_element_type=jnp.float32,
        )
        return (numerator / denominator.T[:, :, None]).astype(jnp.bfloat16)

    block_starts = jnp.arange(block_count, dtype=jnp.int32) * block_len
    heads_out = lax.map(query_block, block_starts).reshape(group_len, head_width)
    attn_rows = lax.psum_scatter(
        jnp.dot(heads_out, out_weight, preferred_element_type=jnp.float32).astype(jnp.bfloat16),
        HEAD,
        scatter_dimension=0,
        tiled=True,
    ).astype(jnp.float32)
    stream = (tokens.astype(jnp.float32) + attn_rows).reshape(local_rows // 4, 4, D)
    average = jnp.sum(stream, axis=2, keepdims=True) / D
    variance = jnp.sum(stream * stream, axis=2, keepdims=True) / D - average * average
    window_rows = ((stream - average) * lax.rsqrt(variance + EPSILON) * merge_gain).astype(
        jnp.bfloat16
    )
    merged_slice = lax.all_to_all(
        window_rows.reshape(local_rows // 4, 4 * D), HEAD, split_axis=1, concat_axis=0, tiled=True
    )
    merged_count = local_rows // 4
    column_terms = jnp.dot(
        merged_slice,
        lax.all_gather(
            lax.all_gather(merge_weight, "tz", axis=1, tiled=True), "tx", axis=1, tiled=True
        ),
        preferred_element_type=jnp.float32,
    )
    projected = lax.psum_scatter(
        column_terms.astype(jnp.bfloat16), HEAD, scatter_dimension=0, tiled=True
    )
    slot_count = max(2, 2 * merged_count // tok_count)
    owner_col = owners[:, 0]
    owner_hot = (owner_col[:, None] == jnp.arange(tok_count, dtype=jnp.int32)[None, :]).astype(
        jnp.int32
    )
    earlier = jnp.cumsum(owner_hot, axis=0, dtype=jnp.int32) - owner_hot
    slot_index = jnp.sum(earlier * owner_hot, axis=1, dtype=jnp.int32)
    target = owner_col * slot_count + slot_index
    select = (
        jnp.arange(tok_count * slot_count, dtype=jnp.int32)[:, None] == target[None, :]
    ).astype(jnp.bfloat16)
    send_rows = jnp.dot(select, projected, preferred_element_type=jnp.float32).astype(jnp.bfloat16)
    send_rows = send_rows.reshape(tok_count, slot_count, -1)
    received = lax.all_to_all(send_rows, TOK, split_axis=0, concat_axis=0, tiled=True)
    return received.reshape(tok_count * slot_count, -1)


def solution(mesh):
    tok_size, head_size = (mesh.shape[name] for name in mesh.axis_names)
    split_mesh = jax.sharding.Mesh(
        mesh.devices.reshape(tok_size // Z_SIZE, Z_SIZE, head_size // 2, 2), TOK + HEAD
    )
    placed = (
        P(TOK + HEAD, None),
        P(),
        P(None, HEAD, None),
        P(HEAD, None),
        P(),
        P(HEAD, TOK),
        P(None, TOK),
        P(TOK),
        P(None, TOK),
        P(TOK),
        P(TOK + HEAD, None),
    )
    return jax.shard_map(
        body, mesh=split_mesh, in_specs=placed, out_specs=P(TOK + HEAD, None), check_vma=False
    )
```

profile of v0, /device:TPU:57, one launch (start us, length us, event | category | flops | bytes accessed | tf_op | source)
XLA Modules:
  0.0 283.4 jit_solution(1939351082981799064)
XLA Ops:
  6.5 1.3 convert_reduce_fusion
  7.8 1.3 fusion.46
  9.1 2.1 fusion.48
  11.2 0.0 all-gather.4.cloned.1.call-update
  11.2 0.0 all-gather.6.cloned.1.call-start
  11.3 0.7 all-gather.6.cloned.1.call-update
  12.0 0.0 reduce-scatter.3.cloned.1.call-start
  12.1 0.7 convert_element_type.65
  12.8 0.8 convert_multiply_fusion.1
  13.5 0.7 broadcast_compare_fusion
  14.2 0.7 broadcast_subtract_fusion
  14.9 0.1 select_reduce_fusion.2
  15.1 1.0 multiply_cosine_fusion.1
  16.0 28.0 %all-gather.4.cloned.1.call-done = bf16[1024,1664]{1,0:T(8,128)(2,1)} async-done(((bf16[128,1664]{1,0:T(8,128)(2,1)}), bf16[1024,1664]{1,0:T(8,128)(2,1)}) %all-gather.4.cloned.1.call-update) | async-done | bytes 3407888 | tf_op jit(solution)/shard_map/all_gather | solution.py:70
  44.1 4.5 %fusion.39 = f32[1024,3,2,104]{0,3,2,1:T(8,128)S(1)} fusion(bf16[3,2,104,1664]{3,2,1,0:T(8,128)(2,1)S(1)} %bitcast.70, bf16[1024,1664]{1,0:T(8,128)(2,1)} %all-gather.4.cloned.1.call-done), kind=kOutput, calls=%fused_computation.27 | convolution fusion | flops 2126512128 | bytes 8040448 | tf_op jit(solution)/shard_map/dot_general | solution.py:69
  48.6 0.2 slice_bitcast_fusion
  48.8 0.2 subtract_convert_fusion.1
  49.0 0.0 copy-start.3
  49.0 0.9 pad_maximum_fusion
  49.9 0.2 multiply_subtract_fusion.1
  50.0 0.9 fusion.49
  50.9 0.8 fusion.50
  51.8 23.2 %while.10 = (s32[]{:T(128)}, bf16[2,512,2,104]{1,3,2,0:T(8,128)(2,1)}, s32[2]{0:T(128)S(1)}, s32[1024]{0:T(1024)S(1)}, pred[1024]{0:T(1024)(128)(4,1)S(1)}, /*in...) while((s32[]{:T(128)}, ...), condition=%wide.region_9.10_spmd, body=%wide.region_6.0_spmd.sunk | while | flops 443762176 | bytes 7069351 | solution.py:109
  51.8 0.6 dynamic_slice.26
  54.2 0.1 dynamic_slice.27
  54.3 0.6 iota_add_fusion.2
  54.9 0.7 fusion.80
  55.6 4.6 %fusion.81 = (f32[2,512]{1,0:T(2,128)S(1)}, bf16[2,512,1024]{2,1,0:T(8,128)(2,1)}) fusion(pred[512,1024]{1,0:T(8,128)(4,1)S(1)} %fusion.80, bf16[1024,2,104]{0,2,1:T(8,128)(2,1)} %get-tuple-element.180, bf16[1024,2,104]{0,2,1:T(8,128)(2,1)} %get-tuple-element.179, s32[]{:T(128)S(6)} %select_n.34), kind=kOutput, calls=%fused_computation.84.clone.1 | convolution fusion | flops 223347712 | bytes 3788804 | tf_op jit(solution)/shard_map/while/body/eval_jaxpr/sub | solution.py:98
  60.2 3.1 %fusion.82 = bf16[2,512,2,104]{1,3,2,0:T(8,128)(2,1)} fusion(bf16[2,512,2,104]{1,3,2,0:T(8,128)(2,1)} %get-tuple-element.164, s32[]{:T(128)} %get-tuple-element.163, bf16[1024,2,104]{0,2,1:T(8,128)(2,1)} %get-tuple-element.181, bf16[2,512,1024]{2,1,0:T(8,128)(2,1)} %get-tuple-element.150, f32[512,2]{0,1:T(2,128)S(1)} %bitcast.80), kind=kOutput, calls=%fused_computation.15.clone.1 | convolution fusion | flops 218316800 | bytes 2740736 | tf_op jit(solution)/shard_map/while/body/eval_jaxpr/hqk,khd->qhd/dot_general | solution.py:100
  63.3 0.6 dynamic_slice.26
  65.8 0.1 dynamic_slice.27
  65.9 0.6 iota_add_fusion.2
  66.5 0.7 fusion.80
  67.2 4.6 %fusion.81 = (f32[2,512]{1,0:T(2,128)S(1)}, bf16[2,512,1024]{2,1,0:T(8,128)(2,1)}) fusion(pred[512,1024]{1,0:T(8,128)(4,1)S(1)} %fusion.80, bf16[1024,2,104]{0,2,1:T(8,128)(2,1)} %get-tuple-element.180, bf16[1024,2,104]{0,2,1:T(8,128)(2,1)} %get-tuple-element.179, s32[]{:T(128)S(6)} %select_n.34), kind=kOutput, calls=%fused_computation.84.clone.1 | convolution fusion | flops 223347712 | bytes 3788804 | tf_op jit(solution)/shard_map/while/body/eval_jaxpr/sub | solution.py:98
  71.8 3.1 %fusion.82 = bf16[2,512,2,104]{1,3,2,0:T(8,128)(2,1)} fusion(bf16[2,512,2,104]{1,3,2,0:T(8,128)(2,1)} %get-tuple-element.164, s32[]{:T(128)} %get-tuple-element.163, bf16[1024,2,104]{0,2,1:T(8,128)(2,1)} %get-tuple-element.181, bf16[2,512,1024]{2,1,0:T(8,128)(2,1)} %get-tuple-element.150, f32[512,2]{0,1:T(2,128)S(1)} %bitcast.80), kind=kOutput, calls=%fused_computation.15.clone.1 | convolution fusion | flops 218316800 | bytes 2740736 | tf_op jit(solution)/shard_map/while/body/eval_jaxpr/hqk,khd->qhd/dot_general | solution.py:100
  74.9 1.5 copy.16
  76.4 0.1 copy.21
  76.5 3.0 %convolution_convert_fusion.2 = bf16[1024,1664]{1,0:T(8,128)(2,1)} fusion(bf16[1024,208]{0,1:T(8,128)(2,1)S(1)} %bitcast.71, bf16[208,1664]{1,0:T(8,128)(2,1)S(1)} %copy-done.2), kind=kOutput, calls=%fused_computation.26 | convolution fusion | flops 710541312 | bytes 4526080 | tf_op jit(solution)/shard_map/dot_general | solution.py:111
  79.4 0.0 reduce-scatter.3.cloned.1.call-update
  79.5 0.0 all-gather.8.cloned.1.call-start
  79.5 6.4 %all-gather.6.cloned.1.call-done = bf16[832,1024]{1,0:T(8,128)(2,1)} async-done(((bf16[832,128]{1,0:T(8,128)(2,1)}), bf16[832,1024]{1,0:T(8,128)(2,1)}) %all-gather.6.cloned.1.call-update) | async-done | bytes 1703952 | tf_op jit(solution)/shard_map/all_gather | solution.py:129
  85.9 0.0 all-gather.8.cloned.1.call-update
  86.0 0.0 reduce-scatter.5.cloned.1.call-start
  86.0 0.1 mul.317
  86.1 43.7 %reduce-scatter.3.cloned.1.call-done = bf16[128,1664]{1,0:T(8,128)(2,1)} async-done(((bf16[1024,1664]{1,0:T(8,128)(2,1)}), bf16[128,1664]{1,0:T(8,128)(2,1)}) %reduce-scatter.3.cloned.1.call-update) | async-done | bytes 426000 | tf_op jit(solution)/shard_map/reduce_scatter | solution.py:110
  129.8 2.1 fusion.53
  131.9 0.1 div.50
  132.0 0.1 div.52
  132.1 0.1 copy.17
  132.2 0.1 copy.19
  132.3 1.4 reshape.306
  133.7 0.3 fusion.45
  134.0 11.9 %all_to_all.21 = bf16[32,8,832]{2,0,1:T(8,128)(2,1)S(1)} all-to-all(bf16[32,8,832]{2,0,1:T(8,128)(2,1)S(1)} %fusion.45), channel_id=1, replica_groups=mesh['tx'=4,'tz'=8,'hy'=4,'hc'=2] {'hy','hc'}, dimensions={1} | all-to-all | bytes 851968 | tf_op jit(solution)/shard_map/all_to_all | solution.py:122
  145.9 58.5 %all-gather.8.cloned.1.call-done = bf16[832,4096]{1,0:T(8,128)(2,1)} async-done(((bf16[832,1024]{1,0:T(8,128)(2,1)}), bf16[832,4096]{1,0:T(8,128)(2,1)}) %all-gather.8.cloned.1.call-update) | async-done | bytes 6815760 | tf_op jit(solution)/shard_map/all_gather | solution.py:128
  204.4 6.8 %convolution_convert_fusion = bf16[256,4096]{1,0:T(8,128)(2,1)} fusion(bf16[256,832]{1,0:T(8,128)(2,1)S(1)} %bitcast.73, bf16[832,4096]{1,0:T(8,128)(2,1)} %all-gather.8.cloned.1.call-done), kind=kOutput, calls=%fused_computation.24 | convolution fusion | flops 1745879040 | bytes 9338880 | tf_op jit(solution)/shard_map/dot_general | solution.py:126
  211.2 0.0 reduce-scatter.5.cloned.1.call-update
  211.2 0.1 fusion.52
  211.3 0.1 reduce_window_sum.11
  211.3 0.2 select_reduce_fusion.3
  211.5 35.4 %reduce-scatter.5.cloned.1.call-done = bf16[32,4096]{1,0:T(8,128)(2,1)} async-done(((bf16[256,4096]{1,0:T(8,128)(2,1)}), bf16[32,4096]{1,0:T(8,128)(2,1)}) %reduce-scatter.5.cloned.1.call-update) | async-done | bytes 262160 | tf_op jit(solution)/shard_map/reduce_scatter | solution.py:133
  247.0 1.2 convolution_convert_fusion.1
  248.2 0.3 reshape.307
  248.5 27.3 %all_to_all.22 = bf16[32,2,4096]{2,1,0:T(2,128)(2,1)S(1)} all-to-all(bf16[32,2,4096]{2,1,0:T(2,128)(2,1)S(1)} %reshape.307), channel_id=1, replica_groups=mesh['tx'=4,'tz'=8,'hy'=4,'hc'=2] {'tx','tz'}, dimensions={0} | all-to-all | bytes 1048576 | tf_op jit(solution)/shard_map/all_to_all | solution.py:149
  275.8 1.0 reshape.308
  (27 shorter events, 0.1 us)
Async XLA Ops:
  6.5 37.5 %copy-start = (bf16[3,208,1664]{2,1,0:T(8,128)(2,1)S(1)}, bf16[3,208,1664]{2,1,0:T(8,128)(2,1)}, u32[]{:S(2)}) copy-start(bf16[3,208,1664]{2,1,0:T(8,128)(2,1)} %param.15) | copy-start | bytes 6230020
  6.5 37.5 %all-gather.4.cloned.1.call-start = ((), (), s32[]{:S(2)}) async-start(), calls=%async_computation.4 | async-start | bytes 3833856 | tf_op jit(solution)/shard_map/all_gather | solution.py:70
  11.2 74.7 %all-gather.6.cloned.1.call-start = ((), (), s32[]{:S(2)}) async-start(), calls=%async_computation.6 | async-start | bytes 1916928 | tf_op jit(solution)/shard_map/all_gather | solution.py:129
  12.0 117.8 %reduce-scatter.3.cloned.1.call-start = ((), (), s32[]{:S(2)}) async-start(), calls=%async_computation.5 | async-start | bytes 3833856 | tf_op jit(solution)/shard_map/reduce_scatter | solution.py:110
  49.0 2.8 copy-start.3
  51.8 24.7 %copy-start.2 = (bf16[208,1664]{1,0:T(8,128)(2,1)S(1)}, bf16[208,1664]{1,0:T(8,128)(2,1)}, u32[]{:S(2)}) copy-start(bf16[208,1664]{1,0:T(8,128)(2,1)} %param.16) | copy-start | bytes 2076676
  79.4 6.6 %copy-start.4 = (f32[1664]{0:T(1024)S(1)}, f32[1664]{0:T(1024)}, u32[]{:S(2)}) copy-start(f32[1664]{0:T(1024)} %param.17) | copy-start | bytes 19972
  79.4 50.4 %copy-start.1 = (bf16[128,1664]{1,0:T(8,128)(2,1)S(1)}, bf16[128,1664]{1,0:T(8,128)(2,1)}, u32[]{:S(2)}) copy-start(bf16[128,1664]{1,0:T(8,128)(2,1)} %param.13) | copy-start | bytes 1277956
  79.5 125.0 %all-gather.8.cloned.1.call-start = ((), (), s32[]{:S(2)}) async-start(), calls=%async_computation.7 | async-start | bytes 8519680 | tf_op jit(solution)/shard_map/all_gather | solution.py:128
  86.0 161.0 %reduce-scatter.5.cloned.1.call-start = ((), (), s32[]{:S(2)}) async-start(), calls=%async_computation.8 | async-start | bytes 2359296 | tf_op jit(solution)/shard_map/reduce_scatter | solution.py:133
  204.4 6.8 %copy-start.5 = (s32[32,1]{0,1:T(1,128)S(1)}, s32[32,1]{0,1:T(1,128)}, u32[]{:S(2)}) copy-start(s32[32,1]{0,1:T(1,128)} %param.23) | copy-start | bytes 388
Sparse Core Ops, SparseCore 0:
  11.3 32.6 all-gather.3
  45.8 40.0 all-gather.5
  88.5 41.2 reduce-scatter.2
  131.5 72.9 all-gather.7
  211.3 35.5 reduce-scatter.4
where the time goes:
time: 284 us; the launch traced here: 283 us
  waiting for transfers between devices  173 us (61%)
  blocking collectives  39.2 us (14%)
  matrix products  30.9 us (11%)
  other arithmetic  16.1 us (6%)
  between operations  13.4 us (5%)
  local copies, waits for them, and re-layouts  7.1 us (2%)
  loops' own time  3.76 us (1%)
    all_gather x1, waiting for transfers between devices, body(): lax.all_gather(lax.all_gather(merge_weight, 'tz', axis=1, tiled=True), 't...  58.5 us
    reduce_scatter x1, waiting for transfers between devices, body(): lax.psum_scatter(jnp.dot(heads_out, out_weight, preferred_element_type=jn...  43.7 us
    reduce_scatter x1, waiting for transfers between devices, body(): lax.psum_scatter(column_terms.astype(jnp.bfloat16), HEAD, scatter_dimensi...  35.4 us
    all_gather x1, waiting for transfers between devices, body(): lax.all_gather(normed, HEAD, axis=0, tiled=True)  28 us
    all_to_all x1, blocking collectives, body(): lax.all_to_all(send_rows, TOK, split_axis=0, concat_axis=0, tiled=True)  27.3 us
    all_to_all x1, blocking collectives, body(): lax.all_to_all(window_rows.reshape(local_rows // 4, 4 * D), HEAD, split_a...  11.9 us
    sub x2, matrix products, query_block(): exponent = jnp.where(allowed[None], jnp.exp(masked - row_top), 0.0)  9.24 us
    dot_general x1, matrix products, body(): jnp.dot(merged_slice, lax.all_gather(lax.all_gather(merge_weight, 'tz', a...  6.76 us
  transfers between devices with their start and end apart: 5, of which 5 were waited for; matrix products, arithmetic and copies ran while one was open for 14% of the time, Pallas kernels for 0%

commit v1 on v0

--- a/solution.py
+++ b/solution.py
@@ -67,7 +67,9 @@
     stacked_weight = qkv_weight.reshape(3 * head_width, D)
     normed = layer_norm(tokens.astype(jnp.float32), attn_gain).astype(jnp.bfloat16)
     projected_rows = lax.dot_general(
-        lax.all_gather(normed, HEAD, axis=0, tiled=True),
+        jnp.concatenate(
+            lax.all_to_all(jnp.stack([normed] * lax.axis_size(HEAD)), HEAD, 0, 0), axis=0
+        ),
         stacked_weight,
         (((1,), (1,)), ((), ())),
         preferred_element_type=jnp.float32,

time: 284 us -> 251 us (0.88)
  waiting for transfers between devices: 173 us -> 134 us
  starting transfers between devices: 0.16 us -> 5.24 us
  other arithmetic: 16.1 us -> 12.6 us
    all_gather x1, waiting for transfers between devices: 58.5 us -> 20.8 us  [body(): lax.all_gather(lax.all_gather(merge_weight, 'tz', axis=1, tiled=True), 't...]
    all_to_all x0 -> x1, waiting for transfers between devices: none -> 36.6 us  [body(): lax.all_to_all(jnp.stack([normed] * lax.axis_size(HEAD)), HEAD, 0, 0)]
    all_gather x1 -> x0, waiting for transfers between devices: 28 us -> none  [body(): lax.all_gather(normed, HEAD, axis=0, tiled=True)]
    all_gather x1, waiting for transfers between devices: 6.42 us -> 0.02 us  [body(): lax.all_gather(merge_weight, 'tz', axis=1, tiled=True)]
    all_to_all x0 -> x1, starting transfers between devices: none -> 5.12 us  [body(): lax.all_to_all(jnp.stack([normed] * lax.axis_size(HEAD)), HEAD, 0, 0)]
    reduce_scatter x1, waiting for transfers between devices: 43.7 us -> 39.9 us  [body(): lax.psum_scatter(jnp.dot(heads_out, out_weight, preferred_element_type=jn...]
  transfers between devices with their start and end apart: 5 -> 5, of which waited for: 5 -> 4; matrix products, arithmetic and copies ran while one was open for 14% -> 15% of each run, Pallas kernels for 0% -> 0%
where the time goes in v1:
time: 251 us; the launch traced here: 250 us
  waiting for transfers between devices  134 us (53%)
  blocking collectives  38.8 us (15%)
  matrix products  30.9 us (12%)
  between operations  15.2 us (6%)
  other arithmetic  12.6 us (5%)
  local copies, waits for them, and re-layouts  9.24 us (4%)
  starting transfers between devices  5.24 us (2%)
  loops' own time  4.18 us (2%)
    reduce_scatter x1, waiting for transfers between devices, body(): lax.psum_scatter(jnp.dot(heads_out, out_weight, preferred_element_type=jn...  39.9 us
    all_to_all x1, waiting for transfers between devices, body(): lax.all_to_all(jnp.stack([normed] * lax.axis_size(HEAD)), HEAD, 0, 0)  36.6 us
    reduce_scatter x1, waiting for transfers between devices, body(): lax.psum_scatter(column_terms.astype(jnp.bfloat16), HEAD, scatter_dimensi...  35.4 us
    all_to_all x1, blocking collectives, body(): lax.all_to_all(send_rows, TOK, split_axis=0, concat_axis=0, tiled=True)  27.2 us
    all_gather x1, waiting for transfers between devices, body(): lax.all_gather(lax.all_gather(merge_weight, 'tz', axis=1, tiled=True), 't...  20.8 us
    all_to_all x1, blocking collectives, body(): lax.all_to_all(window_rows.reshape(local_rows // 4, 4 * D), HEAD, split_a...  11.6 us
    sub x2, matrix products, query_block(): exponent = jnp.where(allowed[None], jnp.exp(masked - row_top), 0.0)  9.23 us
    dot_general x1, matrix products, body(): jnp.dot(merged_slice, lax.all_gather(lax.all_gather(merge_weight, 'tz', a...  6.77 us
  transfers between devices with their start and end apart: 5, of which 4 were waited for; matrix products, arithmetic and copies ran while one was open for 15% of the time, Pallas kernels for 0%

profile of v1, /device:TPU:57, one launch (start us, length us, event | category | flops | bytes accessed | tf_op | source)
XLA Modules:
  0.0 250.3 jit_solution(7336181758455419596)
XLA Ops:
  7.4 0.0 copy-start
  7.4 1.3 convert_reduce_fusion
  8.7 1.3 fusion.44
  9.9 1.3 fusion.46
  11.3 2.0 stack.2
  13.3 5.1 %all-to-all-start = ((bf16[8,128,1664]{2,1,0:T(8,128)(2,1)}), bf16[8,128,1664]{2,1,0:T(8,128)(2,1)}, u32[]{:S(2)}, u32[]{:S(2)}) async-start(bf16[8,128,1664]{2,1,0:T(8,128)(2,1)} %stack.2), calls=%async_computation | async-start | bytes 6815744 | tf_op jit(solution)/shard_map/all_to_all | solution.py:71
  18.4 0.0 all-gather.3.cloned.1.call-start
  18.4 0.7 all-gather.3.cloned.1.call-update
  19.1 0.0 reduce-scatter.3.cloned.1.call-start
  19.2 0.0 copy-done.8
  19.2 0.0 copy-done.3
  19.3 0.1 select_reduce_fusion.2
  19.5 1.0 multiply_cosine_fusion.1
  20.5 36.6 %all-to-all-done = bf16[8,128,1664]{2,1,0:T(8,128)(2,1)} async-done(((bf16[8,128,1664]{2,1,0:T(8,128)(2,1)}), bf16[8,128,1664]{2,1,0:T(8,128)(2,1)}, u32[]{:S(2)}, u32[]{:S(2)}) %all-to-all-start) | async-done | bytes 3407904 | tf_op jit(solution)/shard_map/all_to_all | solution.py:71
  57.1 4.5 %fusion.57 = f32[1024,3,2,104]{0,3,2,1:T(8,128)S(1)} fusion(bf16[1024,1664,1,1]{1,0,3,2:T(8,128)(2,1)} %bitcast.7, bf16[3,2,104,1664]{3,2,1,0:T(8,128)(2,1)S(1)} %bitcast.71), kind=kOutput, calls=%fused_computation.83 | convolution fusion | flops 2126512128 | bytes 8040448 | tf_op jit(solution)/shard_map/dot_general | solution.py:69
  61.6 0.2 slice_bitcast_fusion
  61.8 0.2 subtract_convert_fusion.1
  62.0 0.9 pad_maximum_fusion
  62.9 0.2 multiply_subtract_fusion.1
  63.0 0.9 fusion.47
  63.9 0.8 fusion.48
  64.8 23.8 %while.10 = (s32[]{:T(128)}, bf16[2,512,2,104]{1,3,2,0:T(8,128)(2,1)}, s32[2]{0:T(128)S(1)}, s32[1024]{0:T(1024)S(1)}, pred[1024]{0:T(1024)(128)(4,1)S(1)}, /*in...) while((s32[]{:T(128)}, ...), condition=%wide.region_9.10_spmd, body=%wide.region_6.0_spmd.sunk | while | flops 443762176 | bytes 7069351 | solution.py:111
  64.8 0.7 dynamic_slice.26
  67.5 0.1 dynamic_slice.27
  67.6 0.7 iota_add_fusion.2
  68.3 0.7 fusion.80
  69.0 4.6 %fusion.81 = (f32[2,512]{1,0:T(2,128)S(1)}, bf16[2,512,1024]{2,1,0:T(8,128)(2,1)}) fusion(pred[512,1024]{1,0:T(8,128)(4,1)S(1)} %fusion.80, bf16[1024,2,104]{0,2,1:T(8,128)(2,1)} %get-tuple-element.180, bf16[1024,2,104]{0,2,1:T(8,128)(2,1)} %get-tuple-element.179, s32[]{:T(128)S(6)} %select_n.34), kind=kOutput, calls=%fused_computation.82.clone.1 | convolution fusion | flops 223347712 | bytes 3788804 | tf_op jit(solution)/shard_map/while/body/eval_jaxpr/sub | solution.py:100
  73.6 3.1 %fusion.82 = bf16[2,512,2,104]{1,3,2,0:T(8,128)(2,1)} fusion(bf16[2,512,2,104]{1,3,2,0:T(8,128)(2,1)} %get-tuple-element.164, s32[]{:T(128)} %get-tuple-element.163, bf16[1024,2,104]{0,2,1:T(8,128)(2,1)} %get-tuple-element.181, bf16[2,512,1024]{2,1,0:T(8,128)(2,1)} %get-tuple-element.150, f32[512,2]{0,1:T(2,128)S(1)} %bitcast.81), kind=kOutput, calls=%fused_computation.15.clone.1 | convolution fusion | flops 218316800 | bytes 2740736 | tf_op jit(solution)/shard_map/while/body/eval_jaxpr/hqk,khd->qhd/dot_general | solution.py:102
  76.7 0.7 dynamic_slice.26
  79.4 0.1 dynamic_slice.27
  79.5 0.7 iota_add_fusion.2
  80.2 0.7 fusion.80
  80.9 4.6 %fusion.81 = (f32[2,512]{1,0:T(2,128)S(1)}, bf16[2,512,1024]{2,1,0:T(8,128)(2,1)}) fusion(pred[512,1024]{1,0:T(8,128)(4,1)S(1)} %fusion.80, bf16[1024,2,104]{0,2,1:T(8,128)(2,1)} %get-tuple-element.180, bf16[1024,2,104]{0,2,1:T(8,128)(2,1)} %get-tuple-element.179, s32[]{:T(128)S(6)} %select_n.34), kind=kOutput, calls=%fused_computation.82.clone.1 | convolution fusion | flops 223347712 | bytes 3788804 | tf_op jit(solution)/shard_map/while/body/eval_jaxpr/sub | solution.py:100
  85.5 3.1 %fusion.82 = bf16[2,512,2,104]{1,3,2,0:T(8,128)(2,1)} fusion(bf16[2,512,2,104]{1,3,2,0:T(8,128)(2,1)} %get-tuple-element.164, s32[]{:T(128)} %get-tuple-element.163, bf16[1024,2,104]{0,2,1:T(8,128)(2,1)} %get-tuple-element.181, bf16[2,512,1024]{2,1,0:T(8,128)(2,1)} %get-tuple-element.150, f32[512,2]{0,1:T(2,128)S(1)} %bitcast.81), kind=kOutput, calls=%fused_computation.15.clone.1 | convolution fusion | flops 218316800 | bytes 2740736 | tf_op jit(solution)/shard_map/while/body/eval_jaxpr/hqk,khd->qhd/dot_general | solution.py:102
  88.6 1.4 copy.16
  90.0 0.1 copy.21
  90.1 0.0 copy-done.2
  90.1 3.0 %convolution_convert_fusion.2 = bf16[1024,1664]{1,0:T(8,128)(2,1)} fusion(bf16[1024,208]{0,1:T(8,128)(2,1)S(1)} %bitcast.72, bf16[208,1664]{1,0:T(8,128)(2,1)S(1)} %copy-done.2), kind=kOutput, calls=%fused_computation.26 | convolution fusion | flops 710541312 | bytes 4526080 | tf_op jit(solution)/shard_map/dot_general | solution.py:113
  93.1 0.0 reduce-scatter.3.cloned.1.call-update
  93.1 0.0 all-gather.5.cloned.1.call-start
  93.1 0.0 all-gather.3.cloned.1.call-done
  93.2 0.7 all-gather.5.cloned.1.call-update
  93.8 0.0 reduce-scatter.5.cloned.1.call-start
  93.9 0.1 mul.317
  94.0 39.9 %reduce-scatter.3.cloned.1.call-done = bf16[128,1664]{1,0:T(8,128)(2,1)} async-done(((bf16[1024,1664]{1,0:T(8,128)(2,1)}), bf16[128,1664]{1,0:T(8,128)(2,1)}) %reduce-scatter.3.cloned.1.call-update) | async-done | bytes 426000 | tf_op jit(solution)/shard_map/reduce_scatter | solution.py:112
  133.9 2.1 fusion.51
  136.0 0.1 div.50
  136.1 0.1 div.52
  136.2 0.1 copy.17
  136.3 0.1 copy.19
  136.4 1.4 reshape.312
  137.8 0.3 fusion.43
  138.2 11.6 %all_to_all.26 = bf16[32,8,832]{2,0,1:T(8,128)(2,1)S(1)} all-to-all(bf16[32,8,832]{2,0,1:T(8,128)(2,1)S(1)} %fusion.43), channel_id=1, replica_groups=mesh['tx'=4,'tz'=8,'hy'=4,'hc'=2] {'hy','hc'}, dimensions={1} | all-to-all | bytes 851968 | tf_op jit(solution)/shard_map/all_to_all | solution.py:124
  149.8 20.8 %all-gather.5.cloned.1.call-done = bf16[832,4096]{1,0:T(8,128)(2,1)} async-done(((bf16[832,1024]{1,0:T(8,128)(2,1)}), bf16[832,4096]{1,0:T(8,128)(2,1)}) %all-gather.5.cloned.1.call-update) | async-done | bytes 6815760 | tf_op jit(solution)/shard_map/all_gather | solution.py:130
  170.6 6.8 %convolution_convert_fusion = bf16[256,4096]{1,0:T(8,128)(2,1)} fusion(bf16[256,832]{1,0:T(8,128)(2,1)S(1)} %bitcast.74, bf16[832,4096]{1,0:T(8,128)(2,1)} %all-gather.5.cloned.1.call-done), kind=kOutput, calls=%fused_computation.24 | convolution fusion | flops 1745879040 | bytes 9338880 | tf_op jit(solution)/shard_map/dot_general | solution.py:128
  177.3 0.0 reduce-scatter.5.cloned.1.call-update
  177.4 0.1 fusion.50
  177.4 0.1 reduce_window_sum.11
  177.5 0.2 select_reduce_fusion.3
  177.7 35.4 %reduce-scatter.5.cloned.1.call-done = bf16[32,4096]{1,0:T(8,128)(2,1)} async-done(((bf16[256,4096]{1,0:T(8,128)(2,1)}), bf16[32,4096]{1,0:T(8,128)(2,1)}) %reduce-scatter.5.cloned.1.call-update) | async-done | bytes 262160 | tf_op jit(solution)/shard_map/reduce_scatter | solution.py:135
  213.1 1.2 convolution_convert_fusion.1
  214.3 0.3 reshape.313
  214.7 27.2 %all_to_all.27 = bf16[32,2,4096]{2,1,0:T(2,128)(2,1)S(1)} all-to-all(bf16[32,2,4096]{2,1,0:T(2,128)(2,1)S(1)} %reshape.313), channel_id=1, replica_groups=mesh['tx'=4,'tz'=8,'hy'=4,'hc'=2] {'tx','tz'}, dimensions={0} | all-to-all | bytes 1048576 | tf_op jit(solution)/shard_map/all_to_all | solution.py:151
  241.8 1.0 reshape.314
  (33 shorter events, 0.2 us)
Async XLA Ops:
  7.4 49.7 %copy-start = (bf16[3,208,1664]{2,1,0:T(8,128)(2,1)S(1)}, bf16[3,208,1664]{2,1,0:T(8,128)(2,1)}, u32[]{:S(2)}) copy-start(bf16[3,208,1664]{2,1,0:T(8,128)(2,1)} %param.15) | copy-start | bytes 6230020
  13.3 5.9 %copy-start.8 = (s32[2,4]{1,0:T(2,128)S(1)}, s32[2,4]{1,0:T(2,128)}, u32[]{:S(2)}) copy-start(s32[2,4]{1,0:T(2,128)} %param.19) | copy-start | bytes 100
  13.3 6.0 %copy-start.3 = (s32[1024]{0:T(1024)S(1)}, s32[1024]{0:T(1024)}, u32[]{:S(2)}) copy-start(s32[1024]{0:T(1024)} %param.20) | copy-start | bytes 12292
  13.3 6.1 %copy-start.4 = (s32[2,1024]{1,0:T(2,128)S(1)}, s32[2,1024]{1,0:T(2,128)}, u32[]{:S(2)}) copy-start(s32[2,1024]{1,0:T(2,128)} %param.21) | copy-start | bytes 24580
  13.3 6.2 %copy-start.6 = (s32[1024]{0:T(1024)S(1)}, s32[1024]{0:T(1024)}, u32[]{:S(2)}) copy-start(s32[1024]{0:T(1024)} %param.22) | copy-start | bytes 12292
  13.3 43.8 %all-to-all-start = ((bf16[8,128,1664]{2,1,0:T(8,128)(2,1)}), bf16[8,128,1664]{2,1,0:T(8,128)(2,1)}, u32[]{:S(2)}, u32[]{:S(2)}) async-start(bf16[8,128,1664]{2,1,0:T(8,128)(2,1)} %stack.2), calls=%async_computation | async-start | bytes 6815744 | tf_op jit(solution)/shard_map/all_to_all | solution.py:71
  18.4 74.8 %all-gather.3.cloned.1.call-start = ((), (), s32[]{:S(2)}) async-start(), calls=%async_computation.6 | async-start | bytes 1916928 | tf_op jit(solution)/shard_map/all_gather | solution.py:131
  19.1 114.8 %reduce-scatter.3.cloned.1.call-start = ((), (), s32[]{:S(2)}) async-start(), calls=%async_computation.5 | async-start | bytes 3833856 | tf_op jit(solution)/shard_map/reduce_scatter | solution.py:112
  64.8 25.3 %copy-start.2 = (bf16[208,1664]{1,0:T(8,128)(2,1)S(1)}, bf16[208,1664]{1,0:T(8,128)(2,1)}, u32[]{:S(2)}) copy-start(bf16[208,1664]{1,0:T(8,128)(2,1)} %param.16) | copy-start | bytes 2076676
  93.1 0.8 copy-start.5
  93.1 40.8 %copy-start.1 = (bf16[128,1664]{1,0:T(8,128)(2,1)S(1)}, bf16[128,1664]{1,0:T(8,128)(2,1)}, u32[]{:S(2)}) copy-start(bf16[128,1664]{1,0:T(8,128)(2,1)} %param.13) | copy-start | bytes 1277956
  93.1 77.5 %all-gather.5.cloned.1.call-start = ((), (), s32[]{:S(2)}) async-start(), calls=%async_computation.7 | async-start | bytes 8519680 | tf_op jit(solution)/shard_map/all_gather | solution.py:130
  93.8 119.3 %reduce-scatter.5.cloned.1.call-start = ((), (), s32[]{:S(2)}) async-start(), calls=%async_computation.8 | async-start | bytes 2359296 | tf_op jit(solution)/shard_map/reduce_scatter | solution.py:135
  170.6 6.8 %copy-start.7 = (s32[32,1]{0,1:T(1,128)S(1)}, s32[32,1]{0,1:T(1,128)}, u32[]{:S(2)}) copy-start(s32[32,1]{0,1:T(1,128)} %param.23) | copy-start | bytes 388
Sparse Core Ops, SparseCore 0:
  20.9 41.6 all-gather.2
  95.7 74.8 all-gather.4
Sparse Core Ops, SparseCore 1:
  93.2 40.7 reduce-scatter.2
  177.4 35.6 reduce-scatter.4
